TPU v7x, 32 devices: a whole 2x2x4 slice. The times are simulated.
32 devices in a mesh: tm: 8 (over y, x, core), row: 4 (over z).
Axes of the slice: x: 2, y: 2, z: 4, core: 2. Of those that a mesh axis runs over, the one named last changes fastest.
Arguments:
- section_maps: float32 [8, 1024, 1024], P('tm', 'row'), may hold values from -0.04375 to 1.09375, as said below
- terminal_cost: float32 [512, 512], P('row'), may hold values from -0.075 to 1.075, as said below
- terminal_states: float32 [512, 2048], replicated, may hold values from -6 to 6
Outputs:
- trajectories: float32 [8, 1024, 2048], P('tm', 'row')
- section_cost: float32 [8, 2048], P('tm', 'row')
Inputs may be any that keep to these rules, and one draw needn't show every extreme that they name: `section_maps`: each section map is its diagonal plus small entries off the diagonal. `terminal_cost`: symmetric.
All inputs are finite; a program needn't handle non-finite values.
Results may differ from a plain program's by a relative error of at most 0.0003.
Values sent between devices are 32-bit elements; how exact they have to be, the bound alone decides.
No kernel may reach another device: no remote copies, remote signals or barrier semaphores. Data moves between devices by JAX's collectives and lax.ppermute only.
A program may use at most 64 MiB of HBM per device.

v0:
```python
import jax
import jax.numpy as jnp
from jax import lax
from jax.sharding import PartitionSpec as P


def shifted(block, axis, distance):
    devices = range(lax.axis_size(axis))
    route = [(i - distance, i) for i in devices if i - distance in devices]
    return lax.ppermute(block, axis, route)


def product(left, right):
    return jnp.dot(left, right, precision=lax.Precision.HIGHEST, preferred_element_type=jnp.float32)


def body(section_maps, terminal_cost, terminal_states):
    running = section_maps[0]
    state_dim = running.shape[1] // 2
    tm_count = lax.axis_size("tm")
    tm_place = lax.axis_index("tm")
    for level_index in range((tm_count - 1).bit_length()):
        stride = 1 << level_index
        gathered = lax.all_gather(running, "row", axis=0, tiled=True)
        further = shifted(gathered, "tm", -stride)
        combined = product(running, further)
        running = jnp.where(tm_place + stride < tm_count, combined, running)
    portion = lax.all_gather(terminal_cost, "row", axis=0, tiled=True)
    columns = lax.dynamic_slice_in_dim(running, state_dim, portion.shape[0], 1)
    value_rows = running[:, :state_dim] + product(columns, portion)
    rows_traj = product(value_rows, terminal_states)
    regrouped = lax.all_to_all(rows_traj, "row", split_axis=1, concat_axis=0, tiled=True)
    section_cost = jnp.sum(regrouped[:state_dim] * regrouped[state_dim:], axis=0) / state_dim
    return (rows_traj[None], section_cost[None])


def solution(mesh):
    in_specs = (P("tm", "row", None), P("row", None), P())
    out_specs = (P("tm", "row", None), P("tm", "row"))
    return jax.shard_map(body, mesh=mesh, in_specs=in_specs, out_specs=out_specs, check_vma=False)
```

profile of v0, /device:TPU:0, one launch (start us, length us, event | category | flops | bytes accessed | tf_op | source)
XLA Modules:
  0.0 577.2 jit_solution(18376967483935607676)
XLA Ops:
  7.2 0.0 all-gather.12.cloned.1.call-start
  7.2 0.7 all-gather.12.cloned.1.call-update
  7.9 0.0 all-gather.6.cloned.1.call-start
  7.9 85.1 %all-gather.12.cloned.1.call-done = f32[1,1024,1024]{2,1,0:T(8,128)} async-done(((f32[1,256,1024]{2,1,0:T(8,128)}), f32[1,1024,1024]{2,1,0:T(8,128)}) %all-gather.12.cloned.1.call-update) | async-done | bytes 4194320 | tf_op jit(solution)/shard_map/all_gather | solution.py:24
  93.0 1.3 collective-permute-start
  94.3 8.1 %collective-permute-done = f32[1024,1024]{1,0:T(8,128)} collective-permute-done((f32[1024,1024]{1,0:T(8,128)}, f32[1024,1024]{1,0:T(8,128)}, u32[]{:S(2)}, u32[]{:S(2)}) %collective-permute-start) | collective-permute-done | bytes 4194336 | tf_op jit(solution)/shard_map/ppermute | solution.py:10
  102.4 7.4 %convolution_select_fusion.2 = f32[256,1024]{1,0:T(8,128)} fusion(f32[1024,1024]{1,0:T(8,128)} %collective-permute-done, f32[1,256,1024]{2,1,0:T(8,128)} %param.3, pred[]{:T(512)S(6)} %lt.11), kind=kOutput, calls=%fused_computation.3 | convolution fusion | flops 3221487616 | bytes 6291457 | tf_op jit(solution)/shard_map/dot_general | solution.py:14
  109.9 0.0 all-gather.6.cloned.1.call-update
  109.9 0.0 all-gather.8.cloned.1.call-start
  109.9 119.6 %all-gather.6.cloned.1.call-done = f32[1024,1024]{1,0:T(8,128)} async-done(((f32[256,1024]{1,0:T(8,128)}), f32[1024,1024]{1,0:T(8,128)}) %all-gather.6.cloned.1.call-update) | async-done | bytes 4194320 | tf_op jit(solution)/shard_map/all_gather | solution.py:24
  229.5 1.3 collective-permute-start.1
  230.8 93.1 %collective-permute-done.1 = f32[1024,1024]{1,0:T(8,128)} collective-permute-done((f32[1024,1024]{1,0:T(8,128)}, f32[1024,1024]{1,0:T(8,128)}, u32[]{:S(2)}, u32[]{:S(2)}) %collective-permute-start.1) | collective-permute-done | bytes 4194336 | tf_op jit(solution)/shard_map/ppermute | solution.py:10
  323.9 7.5 %convolution_select_fusion.1 = f32[256,1024]{1,0:T(8,128)} fusion(f32[256,1024]{1,0:T(8,128)} %convolution_select_fusion.2, f32[1024,1024]{1,0:T(8,128)} %collective-permute-done.1, pred[]{:T(512)S(6)} %lt.10), kind=kOutput, calls=%fused_computation.2 | convolution fusion | flops 3221487616 | bytes 6291457 | tf_op jit(solution)/shard_map/dot_general | solution.py:14
  331.5 0.0 all-gather.8.cloned.1.call-update
  331.5 0.0 all-gather.10.cloned.1.call-start
  331.5 79.5 %all-gather.8.cloned.1.call-done = f32[1024,1024]{1,0:T(8,128)} async-done(((f32[256,1024]{1,0:T(8,128)}), f32[1024,1024]{1,0:T(8,128)}) %all-gather.8.cloned.1.call-update) | async-done | bytes 4194320 | tf_op jit(solution)/shard_map/all_gather | solution.py:24
  411.0 1.5 collective-permute-start.2
  412.5 0.0 all-gather.10.cloned.1.call-update
  412.5 92.9 %collective-permute-done.2 = f32[1024,1024]{1,0:T(8,128)} collective-permute-done((f32[1024,1024]{1,0:T(8,128)}, f32[1024,1024]{1,0:T(8,128)}, u32[]{:S(2)}, u32[]{:S(2)}) %collective-permute-start.2) | collective-permute-done | bytes 4194336 | tf_op jit(solution)/shard_map/ppermute | solution.py:10
  505.4 6.6 %convolution_select_fusion = f32[256,1024]{1,0:T(8,128)S(1)} fusion(f32[256,1024]{1,0:T(8,128)} %convolution_select_fusion.1, f32[1024,1024]{1,0:T(8,128)} %collective-permute-done.2, pred[]{:T(512)S(6)} %lt.9), kind=kOutput, calls=%fused_computation.1 | convolution fusion | flops 3221487616 | bytes 6291457 | tf_op jit(solution)/shard_map/dot_general | solution.py:14
  512.0 0.0 all-gather.10.cloned.1.call-done
  512.0 2.3 fusion.2
  514.3 5.5 fusion.4
  519.8 0.0 copy-start
  519.8 0.2 copy.8
  520.0 50.0 %all_to_all.16 = f32[256,4,512]{2,0,1:T(8,128)S(1)} all-to-all(f32[256,4,512]{2,0,1:T(8,128)S(1)} %bitcast.21), channel_id=1, replica_groups=mesh['tm'=8,'row'=4] {'row'}, dimensions={1} | all-to-all | bytes 4194304 | tf_op jit(solution)/shard_map/all_to_all | solution.py:32
  570.0 0.0 copy-done
  570.0 0.1 fusion
  570.1 0.6 broadcast_multiply_fusion
Async XLA Ops:
  7.2 85.9 %all-gather.12.cloned.1.call-start = ((), (), s32[]{:S(2)}) async-start(), calls=%async_computation.4 | async-start | bytes 5242880 | tf_op jit(solution)/shard_map/all_gather | solution.py:24
  7.9 221.6 %all-gather.6.cloned.1.call-start = ((), (), s32[]{:S(2)}) async-start(), calls=%async_computation.1 | async-start | bytes 5242880 | tf_op jit(solution)/shard_map/all_gather | solution.py:24
  93.0 9.4 %collective-permute-start = (f32[1024,1024]{1,0:T(8,128)}, f32[1024,1024]{1,0:T(8,128)}, u32[]{:S(2)}, u32[]{:S(2)}) collective-permute-start(f32[1024,1024]{1,0:T(8,128)} %bitcast.23), channel_id=1, source_target_pairs={{4,0},{8,4},{12,8},{16,12},{20,16},{24,20},{28,24},{5,1},{9,5},{13... | collective-permute-start | bytes 12582920 | tf_op jit(solution)/shard_map/ppermute | solution.py:10
  109.9 301.2 %all-gather.8.cloned.1.call-start = ((), (), s32[]{:S(2)}) async-start(), calls=%async_computation.2 | async-start | bytes 5242880 | tf_op jit(solution)/shard_map/all_gather | solution.py:24
  229.5 94.4 %collective-permute-start.1 = (f32[1024,1024]{1,0:T(8,128)}, f32[1024,1024]{1,0:T(8,128)}, u32[]{:S(2)}, u32[]{:S(2)}) collective-permute-start(f32[1024,1024]{1,0:T(8,128)} %all-gather.6.cloned.1.call-done), channel_id=1, source_target_pairs={{8,0},{12,4},{16,8},{20,12},{24,16},{28,20},{9,1},{13,5},{17,9},{2... | collective-permute-start | bytes 12582920 | tf_op jit(solution)/shard_map/ppermute | solution.py:10
  331.5 180.6 %all-gather.10.cloned.1.call-start = ((), (), s32[]{:S(2)}) async-start(), calls=%async_computation.3 | async-start | bytes 1310720 | tf_op jit(solution)/shard_map/all_gather | solution.py:28
  411.0 94.4 %collective-permute-start.2 = (f32[1024,1024]{1,0:T(8,128)}, f32[1024,1024]{1,0:T(8,128)}, u32[]{:S(2)}, u32[]{:S(2)}) collective-permute-start(f32[1024,1024]{1,0:T(8,128)} %all-gather.8.cloned.1.call-done), channel_id=1, source_target_pairs={{16,0},{20,4},{24,8},{28,12},{17,1},{21,5},{25,9},{29,13},{18,2},{... | collective-permute-start | bytes 12582920 | tf_op jit(solution)/shard_map/ppermute | solution.py:10
  519.8 50.2 %copy-start = (f32[256,2048]{1,0:T(8,128)}, f32[256,2048]{1,0:T(8,128)S(1)}, u32[]{:S(2)}) copy-start(f32[256,2048]{1,0:T(8,128)S(1)} %fusion.4) | copy-start | bytes 6291460
Sparse Core Ops, SparseCore 0:
  9.5 83.4 all-gather.11
  110.0 119.4 all-gather.5
  331.6 79.3 all-gather.7
  412.7 29.3 all-gather.9
where the time goes:
time: 577 us
  waiting for transfers between devices  479 us (83%)
  blocking collectives  50 us (9%)
  matrix products  29.3 us (5%)
  between operations  13.9 us (2%)
    all_gather x3, waiting for transfers between devices, body(): gathered = lax.all_gather(running, 'row', axis=0, tiled=True)  284 us
    ppermute x3, waiting for transfers between devices, shifted(): return lax.ppermute(block, axis, route)  194 us
    all_to_all x1, blocking collectives, body(): lax.all_to_all(rows_traj, 'row', split_axis=1, concat_axis=0, tiled=True)  50 us
    dot_general x5, matrix products, product(): jnp.dot(left, right, precision=lax.Precision.HIGHEST, preferred_element_t...  29.3 us
  transfers between devices with their start and end apart: 7, of which 6 were waited for; matrix products, arithmetic and copies ran while one was open for 1% of the time, Pallas kernels for 0%

commit v1 on v0

--- a/solution.py
+++ b/solution.py
@@ -2,6 +2,28 @@
 import jax.numpy as jnp
 from jax import lax
 from jax.sharding import PartitionSpec as P
+
+
+def joined_along(tiles, dim):
+    dims = list(tiles.shape[1:])
+    dims[dim] *= tiles.shape[0]
+    return jnp.moveaxis(tiles, 0, dim).reshape(dims)
+
+
+def gather_around(shard, axis, dim):
+    peers = lax.axis_size(axis)
+    pairs = [(i, (i + 1) % peers) for i in range(peers)]
+    back = [(b, a) for a, b in pairs]
+    lower, upper = ([], [])
+    for lap in range(peers - 1):
+        if lap % 2 == 0:
+            lower.append(lax.ppermute(lower[-1] if lower else shard, axis, pairs))
+        else:
+            upper.append(lax.ppermute(upper[-1] if upper else shard, axis, back))
+    pieces = jnp.stack([*lower[::-1], shard, *upper])
+    shift = lax.axis_index(axis) - len(lower)
+    pieces = pieces[(jnp.arange(peers) - shift) % peers]
+    return joined_along(pieces, dim)
 
 
 def shifted(block, axis, distance):
@@ -21,7 +43,7 @@
     tm_place = lax.axis_index("tm")
     for level_index in range((tm_count - 1).bit_length()):
         stride = 1 << level_index
-        gathered = lax.all_gather(running, "row", axis=0, tiled=True)
+        gathered = gather_around(running, "row", 0)
         further = shifted(gathered, "tm", -stride)
         combined = product(running, further)
         running = jnp.where(tm_place + stride < tm_count, combined, running)

time: 577 us -> 595 us (1.031)
  waiting for transfers between devices: 479 us -> 438 us
  local copies, waits for them, and re-layouts: 0.21 us -> 33 us
  starting transfers between devices: 4.18 us -> 17 us
  other arithmetic: 0.73 us -> 8.72 us
    all_gather x3 -> x0, waiting for transfers between devices: 284 us -> none  [body(): gathered = lax.all_gather(running, 'row', axis=0, tiled=True)]
    ppermute x0 -> x9, waiting for transfers between devices: none -> 171 us  [the longest x6 121 us: gather_around(): lower.append(lax.ppermute(lower[-1] if lower else shard, axis, pairs))]
    ppermute x3, waiting for transfers between devices: 194 us -> 266 us  [shifted(): return lax.ppermute(block, axis, route)]
    gather x0 -> x6, local copies, waits for them, and re-layouts: none -> 31.2 us  [gather_around(): pieces = pieces[(jnp.arange(peers) - shift) % peers]]
    ppermute x0 -> x9, starting transfers between devices: none -> 12.9 us  [the longest x3 9.71 us: gather_around(): upper.append(lax.ppermute(upper[-1] if upper else shard, axis, back))]
    another operation x0 -> x3, other arithmetic: none -> 7.96 us  [gather_around(): pieces = jnp.stack([*lower[::-1], shard, *upper])]
  transfers between devices with their start and end apart: 7 -> 13, of which waited for: 6 -> 12; matrix products, arithmetic and copies ran while one was open for 1% -> 1% of each run, Pallas kernels for 0% -> 0%
where the time goes in v1:
time: 595 us; the launch traced here: 594 us
  waiting for transfers between devices  438 us (74%)
  blocking collectives  49.7 us (8%)
  matrix products  34 us (6%)
  local copies, waits for them, and re-layouts  33 us (6%)
  starting transfers between devices  17 us (3%)
  between operations  14.2 us (2%)
  other arithmetic  8.72 us (1%)
    ppermute x3, waiting for transfers between devices, shifted(): return lax.ppermute(block, axis, route)  266 us
    ppermute x6, waiting for transfers between devices, gather_around(): lower.append(lax.ppermute(lower[-1] if lower else shard, axis, pairs))  121 us
    ppermute x3, waiting for transfers between devices, gather_around(): upper.append(lax.ppermute(upper[-1] if upper else shard, axis, back))  50.4 us
    all_to_all x1, blocking collectives, body(): lax.all_to_all(rows_traj, 'row', split_axis=1, concat_axis=0, tiled=True)  49.7 us
    dot_general x5, matrix products, product(): jnp.dot(left, right, precision=lax.Precision.HIGHEST, preferred_element_t...  34 us
    gather x6, local copies, waits for them, and re-layouts, gather_around(): pieces = pieces[(jnp.arange(peers) - shift) % peers]  31.2 us
  transfers between devices with their start and end apart: 13, of which 12 were waited for; matrix products, arithmetic and copies ran while one was open for 1% of the time, Pallas kernels for 0%

profile of v1, /device:TPU:0, one launch (start us, length us, event | category | flops | bytes accessed | tf_op | source)
XLA Modules:
  0.0 594.1 jit_solution(13641047911348865043)
XLA Ops:
  7.2 0.0 all-gather.2.cloned.1.call-start
  7.2 1.6 copy.16
  8.8 3.1 collective-permute-start
  11.9 2.1 collective-permute-start.2
  14.0 24.0 %collective-permute-done = f32[256,1024]{0,1:T(8,128)S(1)} collective-permute-done((f32[256,1024]{0,1:T(8,128)S(1)}, f32[256,1024]{0,1:T(8,128)S(1)}, u32[]{:S(2)}, u32[]{:S(2)}) %collective-permute-start) | collective-permute-done | bytes 1048608 | tf_op jit(solution)/shard_map/ppermute | solution.py:20
  38.0 0.0 collective-permute-start.1
  38.0 21.2 %collective-permute-done.2 = f32[256,1024]{0,1:T(8,128)S(1)} collective-permute-done((f32[256,1024]{0,1:T(8,128)S(1)}, f32[256,1024]{0,1:T(8,128)S(1)}, u32[]{:S(2)}, u32[]{:S(2)}) %collective-permute-start.2) | collective-permute-done | bytes 1048608 | tf_op jit(solution)/shard_map/ppermute | solution.py:22
  59.2 22.9 %collective-permute-done.1 = f32[256,1024]{0,1:T(8,128)} collective-permute-done((f32[256,1024]{0,1:T(8,128)S(1)}, f32[256,1024]{0,1:T(8,128)}, u32[]{:S(2)}, u32[]{:S(2)}) %collective-permute-start.1) | collective-permute-done | bytes 1048608 | tf_op jit(solution)/shard_map/ppermute | solution.py:20
  82.2 3.5 pad_maximum_fusion
  85.7 5.0 gather_fusion
  90.6 5.5 copy.18
  96.1 1.3 collective-permute-start.3
  97.4 8.1 %collective-permute-done.3 = f32[1024,1024]{1,0:T(8,128)} collective-permute-done((f32[1024,1024]{1,0:T(8,128)}, f32[1024,1024]{1,0:T(8,128)}, u32[]{:S(2)}, u32[]{:S(2)}) %collective-permute-start.3) | collective-permute-done | bytes 4194336 | tf_op jit(solution)/shard_map/ppermute | solution.py:32
  105.5 0.0 copy-done.1
  105.5 8.5 %fusion = f32[256,1024]{0,1:T(8,128)S(1)} fusion(f32[1024,1024]{1,0:T(8,128)} %collective-permute-done.3, f32[1,256,1024]{2,1,0:T(8,128)S(1)} %copy-done.1, pred[]{:T(512)S(6)} %lt.33, f32[1,256,1024]{1,2,0:T(8,128)S(1)} %copy.16), kind=kOutput, calls=%fused_computation.10 | convolution fusion | flops 3221487616 | bytes 7340033 | tf_op jit(solution)/shard_map/dot_general | solution.py:36
  114.0 0.1 collective-permute-start.4
  114.1 3.8 collective-permute-start.6
  117.9 12.9 %collective-permute-done.4 = f32[256,1024]{0,1:T(8,128)S(1)} collective-permute-done((f32[256,1024]{0,1:T(8,128)S(1)}, f32[256,1024]{0,1:T(8,128)S(1)}, u32[]{:S(2)}, u32[]{:S(2)}) %collective-permute-start.4) | collective-permute-done | bytes 1048608 | tf_op jit(solution)/shard_map/ppermute | solution.py:20
  130.8 0.0 collective-permute-start.5
  130.8 9.4 %collective-permute-done.6 = f32[256,1024]{0,1:T(8,128)S(1)} collective-permute-done((f32[256,1024]{0,1:T(8,128)S(1)}, f32[256,1024]{0,1:T(8,128)S(1)}, u32[]{:S(2)}, u32[]{:S(2)}) %collective-permute-start.6) | collective-permute-done | bytes 1048608 | tf_op jit(solution)/shard_map/ppermute | solution.py:22
  140.2 13.0 %collective-permute-done.5 = f32[256,1024]{0,1:T(8,128)S(1)} collective-permute-done((f32[256,1024]{0,1:T(8,128)S(1)}, f32[256,1024]{0,1:T(8,128)S(1)}, u32[]{:S(2)}, u32[]{:S(2)}) %collective-permute-start.5) | collective-permute-done | bytes 1048608 | tf_op jit(solution)/shard_map/ppermute | solution.py:20
  153.2 2.2 pad_maximum_fusion.1
  155.4 4.9 gather_fusion.1
  160.4 5.4 copy.19
  165.8 1.3 collective-permute-start.7
  167.1 165.5 %collective-permute-done.7 = f32[1024,1024]{1,0:T(8,128)} collective-permute-done((f32[1024,1024]{1,0:T(8,128)}, f32[1024,1024]{1,0:T(8,128)}, u32[]{:S(2)}, u32[]{:S(2)}) %collective-permute-start.7) | collective-permute-done | bytes 4194336 | tf_op jit(solution)/shard_map/ppermute | solution.py:32
  332.6 8.5 %convolution_select_fusion.1 = f32[256,1024]{0,1:T(8,128)S(1)} fusion(f32[256,1024]{0,1:T(8,128)S(1)} %fusion, f32[1024,1024]{1,0:T(8,128)} %collective-permute-done.7, pred[]{:T(512)S(6)} %lt.32), kind=kOutput, calls=%fused_computation.8 | convolution fusion | flops 3221487616 | bytes 6291457 | tf_op jit(solution)/shard_map/dot_general | solution.py:36
  341.1 0.1 collective-permute-start.8
  341.2 3.8 collective-permute-start.10
  345.0 24.1 %collective-permute-done.8 = f32[256,1024]{0,1:T(8,128)S(1)} collective-permute-done((f32[256,1024]{0,1:T(8,128)S(1)}, f32[256,1024]{0,1:T(8,128)S(1)}, u32[]{:S(2)}, u32[]{:S(2)}) %collective-permute-start.8) | collective-permute-done | bytes 1048608 | tf_op jit(solution)/shard_map/ppermute | solution.py:20
  369.1 0.0 collective-permute-start.9
  369.1 19.8 %collective-permute-done.10 = f32[256,1024]{0,1:T(8,128)S(1)} collective-permute-done((f32[256,1024]{0,1:T(8,128)S(1)}, f32[256,1024]{0,1:T(8,128)S(1)}, u32[]{:S(2)}, u32[]{:S(2)}) %collective-permute-start.10) | collective-permute-done | bytes 1048608 | tf_op jit(solution)/shard_map/ppermute | solution.py:22
  388.8 24.2 %collective-permute-done.9 = f32[256,1024]{0,1:T(8,128)S(1)} collective-permute-done((f32[256,1024]{0,1:T(8,128)S(1)}, f32[256,1024]{0,1:T(8,128)S(1)}, u32[]{:S(2)}, u32[]{:S(2)}) %collective-permute-start.9) | collective-permute-done | bytes 1048608 | tf_op jit(solution)/shard_map/ppermute | solution.py:20
  413.1 2.2 pad_maximum_fusion.2
  415.3 5.0 gather_fusion.2
  420.3 5.4 copy.21
  425.7 1.5 collective-permute-start.11
  427.1 0.0 all-gather.2.cloned.1.call-update
  427.2 92.4 %collective-permute-done.11 = f32[1024,1024]{1,0:T(8,128)} collective-permute-done((f32[1024,1024]{1,0:T(8,128)}, f32[1024,1024]{1,0:T(8,128)}, u32[]{:S(2)}, u32[]{:S(2)}) %collective-permute-start.11) | collective-permute-done | bytes 4194336 | tf_op jit(solution)/shard_map/ppermute | solution.py:32
  519.5 8.5 %convolution_select_fusion = f32[256,1024]{0,1:T(8,128)S(1)} fusion(f32[256,1024]{0,1:T(8,128)S(1)} %convolution_select_fusion.1, f32[1024,1024]{1,0:T(8,128)} %collective-permute-done.11, pred[]{:T(512)S(6)} %lt.31), kind=kOutput, calls=%fused_computation.7 | convolution fusion | flops 3221487616 | bytes 6291457 | tf_op jit(solution)/shard_map/dot_general | solution.py:36
  528.1 0.0 all-gather.2.cloned.1.call-done
  528.1 3.0 fusion.3
  531.1 5.5 fusion.5
  536.6 0.0 copy-start
  536.6 0.2 copy.30
  536.8 49.7 %all_to_all.16 = f32[256,4,512]{2,0,1:T(8,128)S(1)} all-to-all(f32[256,4,512]{2,0,1:T(8,128)S(1)} %bitcast.46), channel_id=1, replica_groups=mesh['tm'=8,'row'=4] {'row'}, dimensions={1} | all-to-all | bytes 4194304 | tf_op jit(solution)/shard_map/all_to_all | solution.py:54
  586.5 0.1 fusion.1
  586.7 0.6 broadcast_multiply_fusion
  (4 shorter events, 0.0 us)
Async XLA Ops:
  7.2 520.9 %all-gather.2.cloned.1.call-start = ((), (), s32[]{:S(2)}) async-start(), calls=%async_computation.1 | async-start | bytes 1310720 | tf_op jit(solution)/shard_map/all_gather | solution.py:50
  8.8 29.2 %collective-permute-start = (f32[256,1024]{0,1:T(8,128)S(1)}, f32[256,1024]{0,1:T(8,128)S(1)}, u32[]{:S(2)}, u32[]{:S(2)}) collective-permute-start(f32[256,1024]{0,1:T(8,128)S(1)} %bitcast.41), channel_id=1, source_target_pairs={{0,1},{1,2},{2,3},{3,0},{4,5},{5,6},{6,7},{7,4},{8,9},{9,10},{10,1... | collective-permute-start | bytes 3145736 | tf_op jit(solution)/shard_map/ppermute | solution.py:20
  11.9 47.3 %collective-permute-start.2 = (f32[256,1024]{0,1:T(8,128)S(1)}, f32[256,1024]{0,1:T(8,128)S(1)}, u32[]{:S(2)}, u32[]{:S(2)}) collective-permute-start(f32[256,1024]{0,1:T(8,128)S(1)} %bitcast.42), channel_id=1, source_target_pairs={{1,0},{2,1},{3,2},{0,3},{5,4},{6,5},{7,6},{4,7},{9,8},{10,9},{11,1... | collective-permute-start | bytes 3145736 | tf_op jit(solution)/shard_map/ppermute | solution.py:22
  38.0 44.2 %collective-permute-start.1 = (f32[256,1024]{0,1:T(8,128)S(1)}, f32[256,1024]{0,1:T(8,128)}, u32[]{:S(2)}, u32[]{:S(2)}) collective-permute-start(f32[256,1024]{0,1:T(8,128)S(1)} %collective-permute-done), channel_id=1, source_target_pairs={{0,1},{1,2},{2,3},{3,0},{4,5},{5,6},{6,7},{7,4},{8,9},{9,10},{10,1... | collective-permute-start | bytes 3145736 | tf_op jit(solution)/shard_map/ppermute | solution.py:20
  90.6 14.9 %copy-start.1 = (f32[1,256,1024]{2,1,0:T(8,128)S(1)}, f32[1,256,1024]{2,1,0:T(8,128)}, u32[]{:S(2)}) copy-start(f32[1,256,1024]{2,1,0:T(8,128)} %param.3) | copy-start | bytes 3145732
  96.1 9.4 %collective-permute-start.3 = (f32[1024,1024]{1,0:T(8,128)}, f32[1024,1024]{1,0:T(8,128)}, u32[]{:S(2)}, u32[]{:S(2)}) collective-permute-start(f32[1024,1024]{1,0:T(8,128)} %bitcast.47), channel_id=1, source_target_pairs={{4,0},{8,4},{12,8},{16,12},{20,16},{24,20},{28,24},{5,1},{9,5},{13... | collective-permute-start | bytes 12582920 | tf_op jit(solution)/shard_map/ppermute | solution.py:32
  114.0 16.8 %collective-permute-start.4 = (f32[256,1024]{0,1:T(8,128)S(1)}, f32[256,1024]{0,1:T(8,128)S(1)}, u32[]{:S(2)}, u32[]{:S(2)}) collective-permute-start(f32[256,1024]{0,1:T(8,128)S(1)} %fusion), channel_id=1, source_target_pairs={{0,1},{1,2},{2,3},{3,0},{4,5},{5,6},{6,7},{7,4},{8,9},{9,10},{10,1... | collective-permute-start | bytes 3145736 | tf_op jit(solution)/shard_map/ppermute | solution.py:20
  114.1 26.1 %collective-permute-start.6 = (f32[256,1024]{0,1:T(8,128)S(1)}, f32[256,1024]{0,1:T(8,128)S(1)}, u32[]{:S(2)}, u32[]{:S(2)}) collective-permute-start(f32[256,1024]{0,1:T(8,128)S(1)} %fusion), channel_id=1, source_target_pairs={{1,0},{2,1},{3,2},{0,3},{5,4},{6,5},{7,6},{4,7},{9,8},{10,9},{11,1... | collective-permute-start | bytes 3145736 | tf_op jit(solution)/shard_map/ppermute | solution.py:22
  130.8 22.4 %collective-permute-start.5 = (f32[256,1024]{0,1:T(8,128)S(1)}, f32[256,1024]{0,1:T(8,128)S(1)}, u32[]{:S(2)}, u32[]{:S(2)}) collective-permute-start(f32[256,1024]{0,1:T(8,128)S(1)} %collective-permute-done.4), channel_id=1, source_target_pairs={{0,1},{1,2},{2,3},{3,0},{4,5},{5,6},{6,7},{7,4},{8,9},{9,10},{10,1... | collective-permute-start | bytes 3145736 | tf_op jit(solution)/shard_map/ppermute | solution.py:20
  165.8 166.8 %collective-permute-start.7 = (f32[1024,1024]{1,0:T(8,128)}, f32[1024,1024]{1,0:T(8,128)}, u32[]{:S(2)}, u32[]{:S(2)}) collective-permute-start(f32[1024,1024]{1,0:T(8,128)} %bitcast.49), channel_id=1, source_target_pairs={{8,0},{12,4},{16,8},{20,12},{24,16},{28,20},{9,1},{13,5},{17,9},{2... | collective-permute-start | bytes 12582920 | tf_op jit(solution)/shard_map/ppermute | solution.py:32
  341.1 27.9 %collective-permute-start.8 = (f32[256,1024]{0,1:T(8,128)S(1)}, f32[256,1024]{0,1:T(8,128)S(1)}, u32[]{:S(2)}, u32[]{:S(2)}) collective-permute-start(f32[256,1024]{0,1:T(8,128)S(1)} %convolution_select_fusion.1), channel_id=1, source_target_pairs={{0,1},{1,2},{2,3},{3,0},{4,5},{5,6},{6,7},{7,4},{8,9},{9,10},{10,1... | collective-permute-start | bytes 3145736 | tf_op jit(solution)/shard_map/ppermute | solution.py:20
  341.2 47.6 %collective-permute-start.10 = (f32[256,1024]{0,1:T(8,128)S(1)}, f32[256,1024]{0,1:T(8,128)S(1)}, u32[]{:S(2)}, u32[]{:S(2)}) collective-permute-start(f32[256,1024]{0,1:T(8,128)S(1)} %convolution_select_fusion.1), channel_id=1, source_target_pairs={{1,0},{2,1},{3,2},{0,3},{5,4},{6,5},{7,6},{4,7},{9,8},{10,9},{11,1... | collective-permute-start | bytes 3145736 | tf_op jit(solution)/shard_map/ppermute | solution.py:22
  369.1 44.0 %collective-permute-start.9 = (f32[256,1024]{0,1:T(8,128)S(1)}, f32[256,1024]{0,1:T(8,128)S(1)}, u32[]{:S(2)}, u32[]{:S(2)}) collective-permute-start(f32[256,1024]{0,1:T(8,128)S(1)} %collective-permute-done.8), channel_id=1, source_target_pairs={{0,1},{1,2},{2,3},{3,0},{4,5},{5,6},{6,7},{7,4},{8,9},{9,10},{10,1... | collective-permute-start | bytes 3145736 | tf_op jit(solution)/shard_map/ppermute | solution.py:20
  425.7 93.9 %collective-permute-start.11 = (f32[1024,1024]{1,0:T(8,128)}, f32[1024,1024]{1,0:T(8,128)}, u32[]{:S(2)}, u32[]{:S(2)}) collective-permute-start(f32[1024,1024]{1,0:T(8,128)} %bitcast.48), channel_id=1, source_target_pairs={{16,0},{20,4},{24,8},{28,12},{17,1},{21,5},{25,9},{29,13},{18,2},{... | collective-permute-start | bytes 12582920 | tf_op jit(solution)/shard_map/ppermute | solution.py:32
  536.6 49.9 %copy-start = (f32[256,2048]{1,0:T(8,128)}, f32[256,2048]{1,0:T(8,128)S(1)}, u32[]{:S(2)}) copy-start(f32[256,2048]{1,0:T(8,128)S(1)} %fusion.5) | copy-start | bytes 6291460
Sparse Core Ops, SparseCore 0:
  427.3 29.9 all-gather.1
